TPU v7x, 32 devices: a whole 2x2x4 slice. The times are simulated.
32 devices in a mesh: groups: 2 (over y), dp: 4 (over z), tensor: 4 (over x, core).
Axes of the slice: x: 2, y: 2, z: 4, core: 2. Of those that a mesh axis runs over, the one named last changes fastest.
Arguments:
- inputs: bfloat16 [2048, 8192], P(('groups', 'dp'), 'tensor'), parts along dimension 0, may hold values from -6 to 6
- cotangent: bfloat16 [2048, 8192], P(('groups', 'dp'), 'tensor'), parts along dimension 0, may hold values from -6 to 6
- up_blocks: bfloat16 [256, 64, 3, 256], P('dp', 'tensor'), may hold values from -0.21875 to 0.21875
- down_blocks: bfloat16 [256, 64, 3, 256], P('dp', 'tensor'), may hold values from -0.15625 to 0.15625
- low_left: bfloat16 [128, 8192], P(None, 'tensor'), may hold values from -0.0625 to 0.0625
- low_right: bfloat16 [128, 16384], P(None, 'tensor'), may hold values from -0.5 to 0.5
- up_pattern: int32 [64, 3], P('tensor'), may hold values from 0 to 7
- down_pattern: int32 [64, 3], P('tensor'), may hold values from 0 to 7
Outputs:
- grad_input: bfloat16 [2048, 8192], P(('groups', 'dp'), 'tensor'), parts along dimension 0
- grad_up: float32 [512, 64, 3, 256], P(('groups', 'dp'), 'tensor'), parts along dimension 0
- grad_down: float32 [512, 64, 3, 256], P(('groups', 'dp'), 'tensor'), parts along dimension 0
- grad_left: float32 [256, 8192], P(('groups', 'dp'), 'tensor'), parts along dimension 0
- grad_right: float32 [256, 16384], P(('groups', 'dp'), 'tensor'), parts along dimension 0
There are 2 independent parts, one for each index of `groups`. A program takes and returns all parts, laid end to end along the dimension named above; an argument that names none is the same for every part. Nothing has to cross between parts.
Inputs may be any that keep to these rules, and one draw needn't show every extreme that they name: `up_pattern`: feature block within a slice of 8 blocks. `down_pattern`: feature block within a slice of 8 blocks.
All inputs are finite; a program needn't handle non-finite values.
Results may differ from a plain program's by a relative error of at most 0.02.
Values may be sent and summed in bfloat16 or wider, within the bound.
No kernel may reach another device: no remote copies, remote signals or barrier semaphores. Data moves between devices by JAX's collectives and lax.ppermute only.
A program may use at most 128 MiB of HBM per device.

v0:
```python
import math

import jax
import jax.numpy as jnp
from jax import lax
from jax.sharding import PartitionSpec as P

root_coef = 0.7978845608028654
cubic_coef = 0.044715


def swapped(block, axis, distance):
    count = lax.axis_size(axis)
    route = []
    for low in range(count):
        high = low | 1 << distance
        if high != low and high < count:
            route += [(low, high), (high, low)]
    return lax.ppermute(block, axis, route)


def fetch_share(block):
    group_count = lax.axis_size("groups")
    rows = block.shape[0]
    if group_count == 1 or rows % group_count:
        return lax.all_gather(block, "dp", axis=0, tiled=True)
    share = rows // group_count
    mine = lax.dynamic_slice_in_dim(block, lax.axis_index("groups") * share, share, axis=0)
    return lax.all_gather(mine, "dp", axis=0, tiled=False)


def rotated(values, start):
    count = values.shape[0]
    doubled = jnp.concatenate([values, values], axis=0)
    return lax.dynamic_slice_in_dim(doubled, start % count, count, axis=0)


def swap_shares(fetched, block):
    group_count = lax.axis_size("groups")
    if group_count == 1 or block.shape[0] % group_count:
        return fetched, None
    group = lax.axis_index("groups")
    other = None
    if group_count == 2:
        count = fetched.shape[0]
        me = lax.axis_index("dp")
        send = rotated(fetched, me + 1)[: count - 1]
        share = block.shape[0] // 2
        local = lax.dynamic_slice_in_dim(block, (1 - group) * share, share, axis=0)
        halves = 2 if block.shape[1] % 2 == 0 else 1
        width = block.shape[1] // halves
        other = []
        for half in range(halves):
            got = lax.ppermute(
                send[:, :, half * width : (half + 1) * width], "groups", [(0, 1), (1, 0)]
            )
            piece = jnp.concatenate([got, local[None, :, half * width : (half + 1) * width]], axis=0)
            other.append(rotated(piece, count - 1 - me))
        received = [fetched, jnp.concatenate(other, axis=2)]
    else:
        received = [fetched] + [
            lax.ppermute(
                fetched, "groups", [(g, (g + shift) % group_count) for g in range(group_count)]
            )
            for shift in range(1, group_count)
        ]
    reverse = jnp.stack(received[::-1], axis=1)
    doubled = jnp.concatenate([reverse, reverse], axis=1)
    ordered = lax.dynamic_slice_in_dim(doubled, group_count - 1 - group, group_count, axis=1)
    return ordered.reshape((-1,) + block.shape[1:]), other


def split_rows(values, axis, count):
    rows = values.shape[axis] // count
    return [lax.slice_in_dim(values, d * rows, (d + 1) * rows, axis=axis) for d in range(count)]


def butterfly_sum(values, axis):
    count = lax.axis_size(axis)
    if count & (count - 1):
        return lax.psum(values.astype(jnp.bfloat16), axis).astype(jnp.float32)
    total = values
    distance = 0
    while (1 << distance) < count:
        total = total + swapped(total, axis, distance)
        distance += 1
    return total


def gelu_pair(values):
    inner_arg = root_coef * (values + cubic_coef * values * values * values)
    tangent = jnp.tanh(inner_arg)
    forward = 0.5 * values * (1.0 + tangent)
    slopes = 0.5 * (1.0 + tangent) + 0.5 * values * (1.0 - tangent * tangent) * root_coef * (
        1.0 + 3.0 * cubic_coef * values * values
    )
    return (forward, slopes)


def pick_blocks(slices, pattern, block_size):
    picked = []
    for which_section, source in enumerate(slices):
        shaped = source.reshape(source.shape[0], -1, block_size)
        picked.append(jnp.take(shaped, pattern[:, which_section], axis=1))
    return jnp.stack(picked, axis=2)


def shards(
    inputs, cotangent, up_blocks, down_blocks, low_left, low_right, up_pattern, down_pattern
):
    tokens_here, width_here = inputs.shape
    block_size = up_blocks.shape[3]
    hidden_here = up_blocks.shape[1]
    section_count = up_blocks.shape[2]
    blocks_here = width_here // block_size
    dp_size = lax.axis_size("dp")
    inv_root = 1.0 / math.sqrt(tokens_here * dp_size)
    up_fetched = fetch_share(up_blocks)
    down_fetched = fetch_share(down_blocks)
    up_full, up_other = swap_shares(up_fetched, up_blocks)
    sources = [inputs] + [
        swapped(inputs, "tensor", level_bit) for level_bit in range(section_count - 1)
    ]
    selected = pick_blocks(sources, up_pattern, block_size)
    low_part = lax.dot_general(
        inputs, low_left, (((1,), (1,)), ((), ())), preferred_element_type=jnp.float32
    )
    low_sum = butterfly_sum(low_part, "tensor").astype(jnp.bfloat16)
    right_blocks = low_right.reshape(low_right.shape[0], hidden_here, block_size)
    low_term = jnp.einsum("tr,rhj->htj", low_sum, right_blocks, preferred_element_type=jnp.float32)
    picked = pick_blocks([cotangent] * section_count, down_pattern, block_size)
    if up_other is None:
        sparse = jnp.einsum(
            "thsi,ihsj->htj", selected, up_full, preferred_element_type=jnp.float32
        )
        spans = [(0, hidden_here, sparse)]
    else:
        group = lax.axis_index("groups")
        by_share = selected.reshape(selected.shape[:3] + (dp_size, 2, -1))
        own_rows = lax.dynamic_index_in_dim(by_share, group, 4, keepdims=False)
        other_rows = lax.dynamic_index_in_dim(by_share, 1 - group, 4, keepdims=False)
        own_sum = jnp.einsum(
            "thskr,krhsj->htj", own_rows, up_fetched, preferred_element_type=jnp.float32
        )
        spans = []
        lo = 0
        for piece in up_other:
            hi = lo + piece.shape[2]
            spans.append(
                (
                    lo,
                    hi,
                    own_sum[lo:hi]
                    + jnp.einsum(
                        "thskr,krhsj->htj",
                        other_rows[:, lo:hi],
                        piece,
                        preferred_element_type=jnp.float32,
                    ),
                )
            )
            lo = hi
    hidden_spans, slope_spans, down_spans = [], [], []
    for lo, hi, sparse in spans:
        activated, slopes_here = gelu_pair(sparse + low_term[lo:hi])
        hidden_here_span = activated.astype(jnp.bfloat16)
        hidden_spans.append(hidden_here_span)
        slope_spans.append(slopes_here)
        down_spans.append(
            jnp.stack(
                [
                    jnp.einsum(
                        "htj,thso->hjso", rows, picked[:, lo:hi], preferred_element_type=jnp.float32
                    )
                    for rows in split_rows(hidden_here_span, 2, dp_size)
                ]
            )
        )
    hidden = jnp.concatenate(hidden_spans, axis=0)
    slopes = jnp.concatenate(slope_spans, axis=0)
    down_parts = (jnp.concatenate(down_spans, axis=1) * inv_root).astype(jnp.bfloat16)
    down_parts, down_fetched = lax.optimization_barrier((down_parts, down_fetched))
    down_full, _ = swap_shares(down_fetched, down_blocks)
    down_summed = lax.psum_scatter(down_parts, "dp", scatter_dimension=0, tiled=False)
    grad_hidden = jnp.einsum(
        "thso,jhso->htj", picked, down_full, preferred_element_type=jnp.float32
    )
    grad_blocks = (grad_hidden * slopes).astype(jnp.bfloat16)
    up_parts = jnp.stack(
        [
            jnp.einsum("thsi,htj->hsij", rows, grad_blocks, preferred_element_type=jnp.float32)
            for rows in split_rows(selected, 3, dp_size)
        ]
    )
    slot_ids = jnp.arange(blocks_here, dtype=jnp.int32)

    def section_term(which_section):
        spread = jnp.einsum(
            "htj,ihj->thi",
            grad_blocks,
            up_full[:, :, which_section, :],
            preferred_element_type=jnp.float32,
        )
        placing = (up_pattern[:, which_section][:, None] == slot_ids[None, :]).astype(jnp.float32)
        return jnp.einsum("thi,hd->tdi", spread, placing).reshape(tokens_here, width_here)

    incoming = [
        swapped(section_term(level_bit + 1).astype(jnp.bfloat16), "tensor", level_bit)
        for level_bit in range(section_count - 1)
    ]
    up_parts, down_summed = lax.optimization_barrier(
        ((up_parts * inv_root).astype(jnp.bfloat16), down_summed)
    )
    grad_down = jnp.transpose(down_summed.astype(jnp.float32), (1, 0, 2, 3))
    back_part = jnp.einsum(
        "htj,rhj->tr", grad_blocks, right_blocks, preferred_element_type=jnp.float32
    )
    back_low = butterfly_sum(back_part, "tensor").astype(jnp.bfloat16)
    up_summed = lax.psum_scatter(up_parts, "dp", scatter_dimension=0, tiled=False)
    left_parts = jnp.stack(
        split_rows(
            lax.dot_general(
                back_low, inputs, (((0,), (0,)), ((), ())), preferred_element_type=jnp.float32
            ),
            0,
            dp_size,
        )
    )
    right_parts = jnp.stack(
        split_rows(
            jnp.einsum(
                "tr,htj->rhj", low_sum, grad_blocks, preferred_element_type=jnp.float32
            ).reshape(low_sum.shape[1], -1),
            0,
            dp_size,
        )
    )
    joined = (jnp.concatenate([left_parts, right_parts], axis=2) * inv_root).astype(jnp.bfloat16)
    joined, up_summed, incoming = lax.optimization_barrier((joined, up_summed, incoming))
    joined = lax.psum_scatter(joined, "dp", scatter_dimension=0, tiled=False).astype(jnp.float32)
    grad_up = jnp.transpose(up_summed.astype(jnp.float32), (2, 0, 1, 3))
    own_term = section_term(0)
    for level_bit in range(section_count - 1):
        own_term = own_term + incoming[level_bit].astype(jnp.float32)
    grad_input = (
        own_term + jnp.dot(back_low, low_left, preferred_element_type=jnp.float32)
    ).astype(jnp.bfloat16)
    grad_left = joined[:, :width_here]
    grad_right = joined[:, width_here:]
    return (grad_input, grad_up, grad_down, grad_left, grad_right)


def solution(mesh):
    in_specs = (
        P(("groups", "dp"), "tensor"),
        P(("groups", "dp"), "tensor"),
        P("dp", "tensor", None, None),
        P("dp", "tensor", None, None),
        P(None, "tensor"),
        P(None, "tensor"),
        P("tensor", None),
        P("tensor", None),
    )
    out_specs = (
        P(("groups", "dp"), "tensor"),
        P(("groups", "dp"), "tensor", None, None),
        P(("groups", "dp"), "tensor", None, None),
        P(("groups", "dp"), "tensor"),
        P(("groups", "dp"), "tensor"),
    )
    return jax.shard_map(shards, mesh=mesh, in_specs=in_specs, out_specs=out_specs, check_vma=False)
```

profile of v0, /device:TPU:0, one launch (start us, length us, event | category | flops | bytes accessed | tf_op | source)
XLA Modules:
  0.0 420.2 jit_solution(17545334087164627758)
XLA Ops:
  10.9 3.0 collective-permute-start.3
  21.1 4.1 copy.143
  33.4 3.3 broadcast_select_fusion.2
  41.7 3.3 pad_maximum_fusion
  47.1 4.7 %collective-permute-done.5 = f32[256,128]{1,0:T(8,128)S(1)} collective-permute-done((f32[256,128]{1,0:T(8,128)S(1)}, f32[256,128]{1,0:T(8,128)S(1)}, u32[]{:S(2)}, u32[]{:S(2)}) %collective-permute-start.5) | collective-permute-done | bytes 131104 | tf_op jit(solution)/shard_map/ppermute | solution.py:19
  63.9 3.2 gather_fusion.4
  67.1 4.1 copy.146
  75.8 3.1 copy.131
  87.7 21.5 %collective-permute-done.1 = bf16[3,32,8,3,256]{4,1,3,2,0:T(8,128)(2,1)S(1)} collective-permute-done((bf16[3,32,8,3,256]{4,1,3,2,0:T(8,128)(2,1)S(1)}, bf16[3,32,8,3,256]{4,1,3,2,0:T(8,128)(2,1)S(1)}, u32[]{:S(2)}, u32[]{:S(2)}) %collective-permute-start.1) | collective-permute-done | bytes 1179680 | tf_op jit(solution)/shard_map/ppermute | solution.py:54
  110.2 6.4 %multiply_convert_fusion = (bf16[8,256,256]{1,2,0:T(8,128)(2,1)S(1)}, f32[8,256,256]{1,2,0:T(8,128)}) fusion(f32[16,256,256]{1,2,0:T(8,128)S(1)} %copy-done.27, bf16[4,32,8,3,256]{4,1,3,2,0:T(8,128)(2,1)S(1)} %fusion.73, bf16[256,16,3,4,1,32]{0,5,4,3,1,2:T(8,128)(2,1)S(1)} %get-tuple-element.57, f32[16,256,256]{1,2,0:T(8,128)S(1)} %fusion.15), kind=kOutput, calls=%fused_computation.103 | convolution fusion | flops 413663232 | bytes 12058624 | tf_op jit(solution)/shard_map/thskr,krhsj->htj/dot_general | solution.py:154
  117.3 15.9 %collective-permute-done = bf16[3,32,8,3,256]{4,1,3,2,0:T(8,128)(2,1)S(1)} collective-permute-done((bf16[3,32,8,3,256]{4,1,3,2,0:T(8,128)(2,1)S(1)}, bf16[3,32,8,3,256]{4,1,3,2,0:T(8,128)(2,1)S(1)}, u32[]{:S(2)}, u32[]{:S(2)}) %collective-permute-start) | collective-permute-done | bytes 1179680 | tf_op jit(solution)/shard_map/ppermute | solution.py:54
  136.2 6.1 %multiply_convert_fusion.1 = (bf16[8,256,256]{1,2,0:T(8,128)(2,1)S(1)}, f32[8,256,256]{1,2,0:T(8,128)}) fusion(f32[16,256,256]{1,2,0:T(8,128)S(1)} %copy-done.27, bf16[4,32,8,3,256]{4,1,3,2,0:T(8,128)(2,1)S(1)} %fusion.76, bf16[256,16,3,4,1,32]{0,5,4,3,1,2:T(8,128)(2,1)S(1)} %get-tuple-element.57, f32[16,256,256]{1,2,0:T(8,128)S(1)} %fusion.15), kind=kOutput, calls=%fused_computation.104 | convolution fusion | flops 413663232 | bytes 12058624 | tf_op jit(solution)/shard_map/thskr,krhsj->htj/dot_general | solution.py:154
  144.9 3.8 fusion
  159.5 24.2 %collective-permute-done.7 = bf16[3,32,8,3,256]{4,1,0,3,2:T(8,128)(2,1)S(1)} collective-permute-done((bf16[3,32,8,3,256]{4,1,0,3,2:T(8,128)(2,1)S(1)}, bf16[3,32,8,3,256]{4,1,0,3,2:T(8,128)(2,1)S(1)}, u32[]{:S(2)}, u32[]{:S(2)}) %collective-permute-start.7) | collective-permute-done | bytes 1179680 | tf_op jit(solution)/shard_map/ppermute | solution.py:54
  184.7 22.3 %collective-permute-done.6 = bf16[3,32,8,3,256]{4,1,0,3,2:T(8,128)(2,1)S(1)} collective-permute-done((bf16[3,32,8,3,256]{4,1,0,3,2:T(8,128)(2,1)S(1)}, bf16[3,32,8,3,256]{4,1,0,3,2:T(8,128)(2,1)S(1)}, u32[]{:S(2)}, u32[]{:S(2)}) %collective-permute-start.6) | collective-permute-done | bytes 1179680 | tf_op jit(solution)/shard_map/ppermute | solution.py:54
  208.2 3.7 fusion.4
  212.0 4.9 %fusion.8 = bf16[16,256,256]{1,2,0:T(8,128)(2,1)S(1)} fusion(f32[8,256,256]{1,2,0:T(8,128)S(1)} %copy-done.40, f32[8,256,256]{1,2,0:T(8,128)} %get-tuple-element.70, bf16[256,16,3,256]{3,0,2,1:T(8,128)(2,1)S(1)} %bitcast.286, bf16[256,16,1,256]{3,0,2,1:T(8,128)(2,1)S(1)} %copy-done.15, bf16[256,16,1,256]{3,0,2,1:T(8,128)(2,1)S(1)} %copy-done.17, ...), kind=kOutput, calls=%fused_computation.32 | convolution fusion | flops 1620049920 | bytes 18874368 | tf_op jit(solution)/shard_map/thso,jhso->htj/dot_general | solution.py:185
  220.3 4.1 fusion.1
  224.4 34.6 %reduce-scatter.4.cloned.1.call-done = bf16[1,16,64,3,256]{4,2,3,1,0:T(8,128)(2,1)} async-done(((bf16[4,16,64,3,256]{4,2,3,1,0:T(8,128)(2,1)}), bf16[1,16,64,3,256]{4,2,3,1,0:T(8,128)(2,1)}) %reduce-scatter.4.cloned.1.call-update) | async-done | bytes 1572880 | tf_op jit(solution)/shard_map/reduce_scatter | solution.py:184
  259.3 3.2 copy.134
  262.9 4.6 %fusion.7 = bf16[4,2,32,16,3,256]{5,2,4,3,0,1:T(8,128)(2,1)S(1)} fusion(s32[]{:T(128)S(6)} %select_n.61, bf16[4,1,32,16,3,256]{5,2,4,3,0,1:T(8,128)(2,1)S(1)} %maximum_bitcast_fusion, bf16[4,1,32,16,3,256]{5,2,4,3,0,1:T(8,128)(2,1)S(1)} %copy.134), kind=kLoop, calls=%fused_computation.23 | loop fusion | flops 9437184 | bytes 12582916 | tf_op jit(solution)/shard_map/concatenate | solution.py:68
  267.5 3.9 copy.136
  295.2 4.8 %copy.180 = bf16[256,16,256]{2,1,0:T(8,128)(2,1)} copy(bf16[256,16,256]{0,2,1:T(8,128)(2,1)} %convolution_bitcast_fusion.1) | data formatting | bytes 4194304 | tf_op jit(solution)/shard_map/htj,ihj->thi/transpose | solution.py:198
  306.2 4.5 %copy.183 = bf16[256,16,256]{2,1,0:T(8,128)(2,1)} copy(bf16[256,16,256]{0,2,1:T(8,128)(2,1)} %convolution_bitcast_fusion) | data formatting | bytes 4194304 | tf_op jit(solution)/shard_map/htj,ihj->thi/transpose | solution.py:198
  318.9 21.9 %collective-permute-done.11 = bf16[256,2048]{1,0:T(8,128)(2,1)} collective-permute-done((bf16[256,2048]{1,0:T(8,128)(2,1)}, bf16[256,2048]{1,0:T(8,128)(2,1)}, u32[]{:S(2)}, u32[]{:S(2)}) %collective-permute-start.11) | collective-permute-done | bytes 1048608 | tf_op jit(solution)/shard_map/ppermute | solution.py:19
  340.9 31.6 %reduce-scatter.6.cloned.1.call-done = bf16[1,16,3,64,256]{4,3,2,1,0:T(8,128)(2,1)} async-done(((bf16[4,16,3,64,256]{4,3,2,1,0:T(8,128)(2,1)}), bf16[1,16,3,64,256]{4,3,2,1,0:T(8,128)(2,1)}) %reduce-scatter.6.cloned.1.call-update) | async-done | bytes 1572880 | tf_op jit(solution)/shard_map/reduce_scatter | solution.py:219
  372.5 3.8 convolution_bitcast_fusion.2
  376.3 3.3 copy.165
  382.1 3.5 copy.185
  386.0 3.5 copy.184
  389.5 3.0 add_convert_fusion
  392.5 18.1 %reduce-scatter.8.cloned.1.call-done = bf16[1,32,6144]{2,1,0:T(8,128)(2,1)} async-done(((bf16[4,32,6144]{2,1,0:T(8,128)(2,1)}), bf16[1,32,6144]{2,1,0:T(8,128)(2,1)}) %reduce-scatter.8.cloned.1.call-update) | async-done | bytes 393232 | tf_op jit(solution)/shard_map/reduce_scatter | solution.py:240
  (212 shorter events, 118.9 us)
Async XLA Ops:
  7.2 6.7 %copy-start = (bf16[128,2048]{1,0:T(8,128)(2,1)S(1)}, bf16[128,2048]{1,0:T(8,128)(2,1)}, u32[]{:S(2)}) copy-start(bf16[128,2048]{1,0:T(8,128)(2,1)} %param.14) | copy-start | bytes 1572868
  7.2 68.6 %all-gather.5.cloned.1.call-start = ((), (), s32[]{:S(2)}) async-start(), calls=%async_computation.6 | async-start | bytes 3932160 | tf_op jit(solution)/shard_map/all_gather | solution.py:29
  9.5 139.3 %all-gather.7.cloned.1.call-start = ((), (), s32[]{:S(2)}) async-start(), calls=%async_computation.7 | async-start | bytes 3932160 | tf_op jit(solution)/shard_map/all_gather | solution.py:29
  10.9 43.7 %collective-permute-start.3 = (bf16[256,2048]{0,1:T(8,128)(2,1)}, bf16[256,2048]{0,1:T(8,128)(2,1)}, u32[]{:S(2)}, u32[]{:S(2)}) collective-permute-start(bf16[256,2048]{0,1:T(8,128)(2,1)} %copy.141), channel_id=1, source_target_pairs={{0,2},{2,0},{1,3},{3,1},{4,6},{6,4},{5,7},{7,5},{8,10},{10,8},{9,1... | collective-permute-start | bytes 3145736 | tf_op jit(solution)/shard_map/ppermute | solution.py:19
  13.8 47.1 %collective-permute-start.2 = (bf16[256,2048]{0,1:T(8,128)(2,1)}, bf16[256,2048]{0,1:T(8,128)(2,1)}, u32[]{:S(2)}, u32[]{:S(2)}) collective-permute-start(bf16[256,2048]{0,1:T(8,128)(2,1)} %copy.141), channel_id=1, source_target_pairs={{0,1},{1,0},{2,3},{3,2},{4,5},{5,4},{6,7},{7,6},{8,9},{9,8},{10,11... | collective-permute-start | bytes 3145736 | tf_op jit(solution)/shard_map/ppermute | solution.py:19
  14.3 4.2 %copy-start.37 = (s32[16,3]{0,1:T(4,128)S(1)}, s32[16,3]{0,1:T(4,128)}, u32[]{:S(2)}) copy-start(s32[16,3]{0,1:T(4,128)} %param.16) | copy-start | bytes 580
  14.3 4.2 %copy-start.39 = (s32[16,3]{0,1:T(4,128)S(1)}, s32[16,3]{0,1:T(4,128)}, u32[]{:S(2)}) copy-start(s32[16,3]{0,1:T(4,128)} %param.17) | copy-start | bytes 580
  14.3 31.0 %collective-permute-start.4 = (f32[256,128]{1,0:T(8,128)S(1)}, f32[256,128]{1,0:T(8,128)}, u32[]{:S(2)}, u32[]{:S(2)}) collective-permute-start(f32[256,128]{1,0:T(8,128)S(1)} %fusion.124), channel_id=1, source_target_pairs={{0,1},{1,0},{2,3},{3,2},{4,5},{5,4},{6,7},{7,6},{8,9},{9,8},{10,11... | collective-permute-start | bytes 393224 | tf_op jit(solution)/shard_map/ppermute | solution.py:19
  17.0 242.0 %reduce-scatter.4.cloned.1.call-start = ((), (), s32[]{:S(2)}) async-start(), calls=%async_computation.3 | async-start | bytes 7864320 | tf_op jit(solution)/shard_map/reduce_scatter | solution.py:184
  21.1 4.1 copy-start.35
  37.0 4.7 %copy-start.14 = (bf16[256,16,1,256]{3,0,2,1:T(8,128)(2,1)}, bf16[256,16,1,256]{3,0,2,1:T(8,128)(2,1)S(1)}, u32[]{:S(2)}) copy-start(bf16[256,16,1,256]{3,0,2,1:T(8,128)(2,1)S(1)} %select_bitcast_fusion) | copy-start | bytes 6291460
  41.7 4.7 %copy-start.38 = (s32[16]{0:T(128)S(1)}, s32[16]{0:T(128)}, u32[]{:S(2)}) copy-start(s32[16]{0:T(128)} %get-tuple-element.89) | copy-start | bytes 196
  45.1 6.7 %copy-start.36 = (bf16[128,4096]{1,0:T(8,128)(2,1)S(1)}, bf16[128,4096]{1,0:T(8,128)(2,1)}, u32[]{:S(2)}) copy-start(bf16[128,4096]{1,0:T(8,128)(2,1)} %param.15) | copy-start | bytes 3145732
  46.3 5.5 %collective-permute-start.5 = (f32[256,128]{1,0:T(8,128)S(1)}, f32[256,128]{1,0:T(8,128)S(1)}, u32[]{:S(2)}, u32[]{:S(2)}) collective-permute-start(f32[256,128]{1,0:T(8,128)S(1)} %add.125), channel_id=1, source_target_pairs={{0,2},{2,0},{1,3},{3,1},{4,6},{6,4},{5,7},{7,5},{8,10},{10,8},{9,1... | collective-permute-start | bytes 393224 | tf_op jit(solution)/shard_map/ppermute | solution.py:19
  60.9 10.3 %copy-start.3 = (bf16[16,256,256]{1,2,0:T(8,128)(2,1)}, bf16[16,256,256]{1,2,0:T(8,128)(2,1)S(1)}, u32[]{:S(2)}) copy-start(bf16[16,256,256]{1,2,0:T(8,128)(2,1)S(1)} %copy.149) | copy-start | bytes 6291460
  80.3 28.9 %collective-permute-start.1 = (bf16[3,32,8,3,256]{4,1,3,2,0:T(8,128)(2,1)S(1)}, bf16[3,32,8,3,256]{4,1,3,2,0:T(8,128)(2,1)S(1)}, u32[]{:S(2)}, u32[]{:S(2)}) collective-permute-start(bf16[3,32,8,3,256]{4,1,3,2,0:T(8,128)(2,1)S(1)} %get-tuple-element.64), channel_id=1, source_target_pairs={{0,16},{16,0},{1,17},{17,1},{2,18},{18,2},{3,19},{19,3},{4,20},{20... | collective-permute-start | bytes 3538952 | tf_op jit(solution)/shard_map/ppermute | solution.py:54
  83.8 49.4 %collective-permute-start = (bf16[3,32,8,3,256]{4,1,3,2,0:T(8,128)(2,1)S(1)}, bf16[3,32,8,3,256]{4,1,3,2,0:T(8,128)(2,1)S(1)}, u32[]{:S(2)}, u32[]{:S(2)}) collective-permute-start(bf16[3,32,8,3,256]{4,1,3,2,0:T(8,128)(2,1)S(1)} %get-tuple-element.63), channel_id=1, source_target_pairs={{0,16},{16,0},{1,17},{17,1},{2,18},{18,2},{3,19},{19,3},{4,20},{20... | collective-permute-start | bytes 3538952 | tf_op jit(solution)/shard_map/ppermute | solution.py:54
  85.4 24.9 %copy-start.27 = (f32[16,256,256]{1,2,0:T(8,128)S(1)}, f32[16,256,256]{1,2,0:T(8,128)}, u32[]{:S(2)}) copy-start(f32[16,256,256]{1,2,0:T(8,128)} %convolution_bitcast_fusion.3) | copy-start | bytes 12582916
  109.2 7.5 %slice-start = ((s8[6291456]{0:T(1024)(128)(4,1)}), s8[4194304]{0:T(1024)(128)(4,1)S(1)}, s32[]{:S(2)}) async-start(s8[6291456]{0:T(1024)(128)(4,1)} %bitcast.274), calls=%async_computation.8 | async-start | bytes 8388608
  110.2 6.4 %copy-start.23 = (bf16[4,32,8,3,256]{4,1,3,2,0:T(8,128)(2,1)}, bf16[4,32,8,3,256]{4,1,3,2,0:T(8,128)(2,1)S(1)}, u32[]{:S(2)}) copy-start(bf16[4,32,8,3,256]{4,1,3,2,0:T(8,128)(2,1)S(1)} %fusion.73) | copy-start | bytes 4718596
  110.2 6.4 %slice-start.1 = ((s8[6291456]{0:T(1024)(128)(4,1)}), s8[2097152]{0:T(1024)(128)(4,1)S(1)}, s32[]{:S(2)}) async-start(s8[6291456]{0:T(1024)(128)(4,1)} %bitcast.274), calls=%async_computation.9 | async-start | bytes 4194304
  148.8 223.7 %reduce-scatter.6.cloned.1.call-start = ((), (), s32[]{:S(2)}) async-start(), calls=%async_computation.4 | async-start | bytes 7864320 | tf_op jit(solution)/shard_map/reduce_scatter | solution.py:219
  154.8 28.9 %collective-permute-start.7 = (bf16[3,32,8,3,256]{4,1,0,3,2:T(8,128)(2,1)S(1)}, bf16[3,32,8,3,256]{4,1,0,3,2:T(8,128)(2,1)S(1)}, u32[]{:S(2)}, u32[]{:S(2)}) collective-permute-start(bf16[3,32,8,3,256]{4,1,0,3,2:T(8,128)(2,1)S(1)} %get-tuple-element.62), channel_id=1, source_target_pairs={{0,16},{16,0},{1,17},{17,1},{2,18},{18,2},{3,19},{19,3},{4,20},{20... | collective-permute-start | bytes 3538952 | tf_op jit(solution)/shard_map/ppermute | solution.py:54
  156.6 50.4 %collective-permute-start.6 = (bf16[3,32,8,3,256]{4,1,0,3,2:T(8,128)(2,1)S(1)}, bf16[3,32,8,3,256]{4,1,0,3,2:T(8,128)(2,1)S(1)}, u32[]{:S(2)}, u32[]{:S(2)}) collective-permute-start(bf16[3,32,8,3,256]{4,1,0,3,2:T(8,128)(2,1)S(1)} %get-tuple-element.61), channel_id=1, source_target_pairs={{0,16},{16,0},{1,17},{17,1},{2,18},{18,2},{3,19},{19,3},{4,20},{20... | collective-permute-start | bytes 3538952 | tf_op jit(solution)/shard_map/ppermute | solution.py:54
  208.2 3.8 copy-start.15
  259.0 151.6 %reduce-scatter.8.cloned.1.call-start = ((), (), s32[]{:S(2)}) async-start(), calls=%async_computation.5 | async-start | bytes 1966080 | tf_op jit(solution)/shard_map/reduce_scatter | solution.py:240
  292.9 17.8 %collective-permute-start.8 = (f32[256,128]{1,0:T(8,128)S(1)}, f32[256,128]{1,0:T(8,128)S(1)}, u32[]{:S(2)}, u32[]{:S(2)}) collective-permute-start(f32[256,128]{1,0:T(8,128)S(1)} %convolution_bitcast_fusion.4), channel_id=1, source_target_pairs={{0,1},{1,0},{2,3},{3,2},{4,5},{5,4},{6,7},{7,6},{8,9},{9,8},{10,11... | collective-permute-start | bytes 393224 | tf_op jit(solution)/shard_map/ppermute | solution.py:19
  300.0 4.0 copy-start.9
  303.5 15.4 %collective-permute-start.10 = (bf16[256,2048]{1,0:T(8,128)(2,1)}, bf16[256,2048]{1,0:T(8,128)(2,1)}, u32[]{:S(2)}, u32[]{:S(2)}) collective-permute-start(bf16[256,2048]{1,0:T(8,128)(2,1)} %bitcast.131), channel_id=1, source_target_pairs={{0,1},{1,0},{2,3},{3,2},{4,5},{5,4},{6,7},{7,6},{8,9},{9,8},{10,11... | collective-permute-start | bytes 3145736 | tf_op jit(solution)/shard_map/ppermute | solution.py:19
  310.8 5.5 %collective-permute-start.9 = (f32[256,128]{1,0:T(8,128)S(1)}, f32[256,128]{1,0:T(8,128)S(1)}, u32[]{:S(2)}, u32[]{:S(2)}) collective-permute-start(f32[256,128]{1,0:T(8,128)S(1)} %add.138), channel_id=1, source_target_pairs={{0,2},{2,0},{1,3},{3,1},{4,6},{6,4},{5,7},{7,5},{8,10},{10,8},{9,1... | collective-permute-start | bytes 393224 | tf_op jit(solution)/shard_map/ppermute | solution.py:19
  312.4 4.0 copy-start.8
  315.8 25.1 %collective-permute-start.11 = (bf16[256,2048]{1,0:T(8,128)(2,1)}, bf16[256,2048]{1,0:T(8,128)(2,1)}, u32[]{:S(2)}, u32[]{:S(2)}) collective-permute-start(bf16[256,2048]{1,0:T(8,128)(2,1)} %bitcast.133), channel_id=1, source_target_pairs={{0,2},{2,0},{1,3},{3,1},{4,6},{6,4},{5,7},{7,5},{8,10},{10,8},{9,1... | collective-permute-start | bytes 3145736 | tf_op jit(solution)/shard_map/ppermute | solution.py:19
  (28 other events, 69.1 us)
Sparse Core Ops, SparseCore 0:
  9.6 66.1 all-gather.4
  77.4 62.0 all-gather.6
  148.9 110.0 reduce-scatter.3
  261.2 111.2 reduce-scatter.5
  374.6 35.9 reduce-scatter.7
where the time goes:
time: 427 us; the launch traced here: 420 us
  waiting for transfers between devices  196 us (46%)
  local copies, waits for them, and re-layouts  104 us (24%)
  matrix products  50.7 us (12%)
  other arithmetic  41.3 us (10%)
  between operations  15.1 us (4%)
  starting transfers between devices  13 us (3%)
    ppermute x4, waiting for transfers between devices, swap_shares(): lax.ppermute(send[:, :, half * width:(half + 1) * width], 'groups', [(0,...  83.8 us
    reduce_scatter x1, waiting for transfers between devices, shards(): lax.psum_scatter(down_parts, 'dp', scatter_dimension=0, tiled=False)  34.6 us
    reduce_scatter x1, waiting for transfers between devices, shards(): lax.psum_scatter(up_parts, 'dp', scatter_dimension=0, tiled=False)  31.6 us
    ppermute x8, waiting for transfers between devices, swapped(): return lax.ppermute(block, axis, route)  26.6 us
    gather x9, local copies, waits for them, and re-layouts, pick_blocks(): picked.append(jnp.take(shaped, pattern[:, which_section], axis=1))  24.2 us
    unnamed x93, local copies, waits for them, and re-layouts  22.5 us
    reduce_scatter x1, waiting for transfers between devices, shards(): lax.psum_scatter(joined, 'dp', scatter_dimension=0, tiled=False)  18.1 us
    transpose x3, local copies, waits for them, and re-layouts, section_term(): jnp.einsum('htj,ihj->thi', grad_blocks, up_full[:, :, which_section, :],...  12.7 us
  transfers between devices with their start and end apart: 17, of which 10 were waited for; matrix products, arithmetic and copies ran while one was open for 43% of the time, Pallas kernels for 0%

commit v1 on v0

--- a/solution.py
+++ b/solution.py
@@ -47,7 +47,7 @@
         send = rotated(fetched, me + 1)[: count - 1]
         share = block.shape[0] // 2
         local = lax.dynamic_slice_in_dim(block, (1 - group) * share, share, axis=0)
-        halves = 2 if block.shape[1] % 2 == 0 else 1
+        halves = 4 if block.shape[1] % 4 == 0 else 1
         width = block.shape[1] // halves
         other = []
         for half in range(halves):

time: 427 us -> 426 us (level)
  waiting for transfers between devices: 196 us -> 184 us
  local copies, waits for them, and re-layouts: 104 us -> 109 us
    ppermute x4 -> x8, waiting for transfers between devices: 83.8 us -> 74.5 us  [swap_shares(): lax.ppermute(send[:, :, half * width:(half + 1) * width], 'groups', [(0,...]
    dot_general x2 -> x4, matrix products: 12.5 us -> 14.2 us  [shards(): jnp.einsum('thskr,krhsj->htj', other_rows[:, lo:hi], piece, preferred_ele...]
    unnamed x93 -> x103, local copies, waits for them, and re-layouts: 22.5 us -> 21.5 us
  transfers between devices with their start and end apart: 17 -> 21, of which waited for: 10 -> 13; matrix products, arithmetic and copies ran while one was open for 43% -> 46% of each run, Pallas kernels for 0% -> 0%
where the time goes in v1:
time: 426 us; the launch traced here: 419 us
  waiting for transfers between devices  184 us (43%)
  local copies, waits for them, and re-layouts  109 us (26%)
  matrix products  54.8 us (13%)
  other arithmetic  41.4 us (10%)
  starting transfers between devices  15.2 us (4%)
  between operations  15.2 us (4%)
    ppermute x8, waiting for transfers between devices, swap_shares(): lax.ppermute(send[:, :, half * width:(half + 1) * width], 'groups', [(0,...  74.5 us
    reduce_scatter x1, waiting for transfers between devices, shards(): lax.psum_scatter(down_parts, 'dp', scatter_dimension=0, tiled=False)  32.2 us
    reduce_scatter x1, waiting for transfers between devices, shards(): lax.psum_scatter(up_parts, 'dp', scatter_dimension=0, tiled=False)  31.2 us
    ppermute x8, waiting for transfers between devices, swapped(): return lax.ppermute(block, axis, route)  28 us
    gather x9, local copies, waits for them, and re-layouts, pick_blocks(): picked.append(jnp.take(shaped, pattern[:, which_section], axis=1))  26.5 us
    unnamed x103, local copies, waits for them, and re-layouts  21.5 us
    reduce_scatter x1, waiting for transfers between devices, shards(): lax.psum_scatter(joined, 'dp', scatter_dimension=0, tiled=False)  18 us
    dot_general x4, matrix products, shards(): jnp.einsum('thskr,krhsj->htj', other_rows[:, lo:hi], piece, preferred_ele...  14.2 us
  transfers between devices with their start and end apart: 21, of which 13 were waited for; matrix products, arithmetic and copies ran while one was open for 46% of the time, Pallas kernels for 0%

profile of v1, /device:TPU:0, one launch (start us, length us, event | category | flops | bytes accessed | tf_op | source)
XLA Modules:
  0.0 419.5 jit_solution(9847797632983829302)
XLA Ops:
  20.4 4.0 copy.163
  43.5 5.3 %collective-permute-done.7 = f32[256,128]{1,0:T(8,128)S(1)} collective-permute-done((f32[256,128]{1,0:T(8,128)S(1)}, f32[256,128]{1,0:T(8,128)S(1)}, u32[]{:S(2)}, u32[]{:S(2)}) %collective-permute-start.7) | collective-permute-done | bytes 131104 | tf_op jit(solution)/shard_map/ppermute | solution.py:19
  48.9 4.0 convolution_bitcast_fusion.3
  58.3 3.9 copy.169
  67.7 4.1 copy.166
  91.2 8.7 %collective-permute-done.3 = bf16[3,32,4,3,256]{4,1,3,2,0:T(8,128)(2,1)S(1)} collective-permute-done((bf16[3,32,4,3,256]{4,1,3,2,0:T(8,128)(2,1)S(1)}, bf16[3,32,4,3,256]{4,1,3,2,0:T(8,128)(2,1)S(1)}, u32[]{:S(2)}, u32[]{:S(2)}) %collective-permute-start.3) | collective-permute-done | bytes 589856 | tf_op jit(solution)/shard_map/ppermute | solution.py:54
  100.3 3.4 multiply_convert_fusion
  105.4 7.1 %collective-permute-done.2 = bf16[3,32,4,3,256]{4,1,3,2,0:T(8,128)(2,1)S(1)} collective-permute-done((bf16[3,32,4,3,256]{4,1,3,2,0:T(8,128)(2,1)S(1)}, bf16[3,32,4,3,256]{4,1,3,2,0:T(8,128)(2,1)S(1)}, u32[]{:S(2)}, u32[]{:S(2)}) %collective-permute-start.2) | collective-permute-done | bytes 589856 | tf_op jit(solution)/shard_map/ppermute | solution.py:54
  113.0 3.9 multiply_convert_fusion.1
  118.4 6.7 %collective-permute-done.1 = bf16[3,32,4,3,256]{4,1,3,2,0:T(8,128)(2,1)S(1)} collective-permute-done((bf16[3,32,4,3,256]{4,1,3,2,0:T(8,128)(2,1)S(1)}, bf16[3,32,4,3,256]{4,1,3,2,0:T(8,128)(2,1)S(1)}, u32[]{:S(2)}, u32[]{:S(2)}) %collective-permute-start.1) | collective-permute-done | bytes 589856 | tf_op jit(solution)/shard_map/ppermute | solution.py:54
  125.6 3.5 multiply_convert_fusion.2
  129.1 7.0 %collective-permute-done = bf16[3,32,4,3,256]{4,1,3,2,0:T(8,128)(2,1)S(1)} collective-permute-done((bf16[3,32,4,3,256]{4,1,3,2,0:T(8,128)(2,1)S(1)}, bf16[3,32,4,3,256]{4,1,3,2,0:T(8,128)(2,1)S(1)}, u32[]{:S(2)}, u32[]{:S(2)}) %collective-permute-start) | collective-permute-done | bytes 589856 | tf_op jit(solution)/shard_map/ppermute | solution.py:54
  138.2 3.4 multiply_convert_fusion.3
  143.2 3.8 fusion
  160.1 11.0 %collective-permute-done.11 = bf16[3,32,4,3,256]{4,1,0,3,2:T(8,128)(2,1)S(1)} collective-permute-done((bf16[3,32,4,3,256]{4,1,0,3,2:T(8,128)(2,1)S(1)}, bf16[3,32,4,3,256]{4,1,0,3,2:T(8,128)(2,1)S(1)}, u32[]{:S(2)}, u32[]{:S(2)}) %collective-permute-start.11) | collective-permute-done | bytes 589856 | tf_op jit(solution)/shard_map/ppermute | solution.py:54
  171.7 12.2 %collective-permute-done.10 = bf16[3,32,4,3,256]{4,1,0,3,2:T(8,128)(2,1)S(1)} collective-permute-done((bf16[3,32,4,3,256]{4,1,0,3,2:T(8,128)(2,1)S(1)}, bf16[3,32,4,3,256]{4,1,0,3,2:T(8,128)(2,1)S(1)}, u32[]{:S(2)}, u32[]{:S(2)}) %collective-permute-start.10) | collective-permute-done | bytes 589856 | tf_op jit(solution)/shard_map/ppermute | solution.py:54
  184.3 12.2 %collective-permute-done.9 = bf16[3,32,4,3,256]{4,1,0,3,2:T(8,128)(2,1)S(1)} collective-permute-done((bf16[3,32,4,3,256]{4,1,0,3,2:T(8,128)(2,1)S(1)}, bf16[3,32,4,3,256]{4,1,0,3,2:T(8,128)(2,1)S(1)}, u32[]{:S(2)}, u32[]{:S(2)}) %collective-permute-start.9) | collective-permute-done | bytes 589856 | tf_op jit(solution)/shard_map/ppermute | solution.py:54
  196.9 9.7 %collective-permute-done.8 = bf16[3,32,4,3,256]{4,1,0,3,2:T(8,128)(2,1)S(1)} collective-permute-done((bf16[3,32,4,3,256]{4,1,0,3,2:T(8,128)(2,1)S(1)}, bf16[3,32,4,3,256]{4,1,0,3,2:T(8,128)(2,1)S(1)}, u32[]{:S(2)}, u32[]{:S(2)}) %collective-permute-start.8) | collective-permute-done | bytes 589856 | tf_op jit(solution)/shard_map/ppermute | solution.py:54
  207.7 5.1 %fusion.4 = bf16[4,2,32,16,3,256]{5,2,1,0,4,3:T(8,128)(2,1)} fusion(s32[]{:T(128)S(6)} %select_n.73, bf16[4,1,32,16,3,256]{5,2,1,0,4,3:T(8,128)(2,1)S(1)} %maximum_bitcast_fusion.1, bf16[4,1,32,16,3,256]{5,2,1,0,4,3:T(8,128)(2,1)S(1)} %bitcast.395), kind=kLoop, calls=%fused_computation.20 | loop fusion | flops 9437184 | bytes 12582916 | tf_op jit(solution)/shard_map/concatenate | solution.py:68
  213.5 5.0 %fusion.8 = bf16[16,256,256]{1,2,0:T(8,128)(2,1)S(1)} fusion(f32[4,256,256]{1,2,0:T(8,128)S(1)} %copy-done.41, f32[4,256,256]{1,2,0:T(8,128)S(1)} %copy-done.42, f32[4,256,256]{1,2,0:T(8,128)S(1)} %copy-done.43, f32[4,256,256]{1,2,0:T(8,128)} %get-tuple-element.86, bf16[256,16,3,256]{3,0,2,1:T(8,128)(2,1)} %bitcast.404, ...), kind=kOutput, calls=%fused_computation.32 | convolution fusion | flops 1622147072 | bytes 18874368 | tf_op jit(solution)/shard_map/thso,jhso->htj/dot_general | solution.py:185
  221.9 4.2 fusion.1
  226.1 32.2 %reduce-scatter.4.cloned.1.call-done = bf16[1,16,64,3,256]{4,2,3,1,0:T(8,128)(2,1)} async-done(((bf16[4,16,64,3,256]{4,2,3,1,0:T(8,128)(2,1)}), bf16[1,16,64,3,256]{4,2,3,1,0:T(8,128)(2,1)}) %reduce-scatter.4.cloned.1.call-update) | async-done | bytes 1572880 | tf_op jit(solution)/shard_map/reduce_scatter | solution.py:184
  262.4 4.6 %fusion.7 = bf16[4,2,32,16,3,256]{5,2,4,3,0,1:T(8,128)(2,1)S(1)} fusion(s32[]{:T(128)S(6)} %select_n.73, bf16[4,1,32,16,3,256]{5,2,4,3,0,1:T(8,128)(2,1)S(1)} %maximum_bitcast_fusion, bf16[4,1,32,16,3,256]{5,2,4,3,0,1:T(8,128)(2,1)S(1)} %copy.154), kind=kLoop, calls=%fused_computation.23 | loop fusion | flops 9437184 | bytes 12582916 | tf_op jit(solution)/shard_map/concatenate | solution.py:68
  267.0 3.9 copy.156
  294.9 4.8 %copy.204 = bf16[256,16,256]{2,1,0:T(8,128)(2,1)} copy(bf16[256,16,256]{0,2,1:T(8,128)(2,1)} %convolution_bitcast_fusion.1) | data formatting | bytes 4194304 | tf_op jit(solution)/shard_map/htj,ihj->thi/transpose | solution.py:198
  306.0 4.6 %copy.207 = bf16[256,16,256]{2,1,0:T(8,128)(2,1)} copy(bf16[256,16,256]{0,2,1:T(8,128)(2,1)} %convolution_bitcast_fusion) | data formatting | bytes 4194304 | tf_op jit(solution)/shard_map/htj,ihj->thi/transpose | solution.py:198
  317.9 22.7 %collective-permute-done.15 = bf16[256,2048]{1,0:T(8,128)(2,1)} collective-permute-done((bf16[256,2048]{1,0:T(8,128)(2,1)}, bf16[256,2048]{1,0:T(8,128)(2,1)}, u32[]{:S(2)}, u32[]{:S(2)}) %collective-permute-start.15) | collective-permute-done | bytes 1048608 | tf_op jit(solution)/shard_map/ppermute | solution.py:19
  340.6 31.2 %reduce-scatter.6.cloned.1.call-done = bf16[1,16,3,64,256]{4,3,2,1,0:T(8,128)(2,1)} async-done(((bf16[4,16,3,64,256]{4,3,2,1,0:T(8,128)(2,1)}), bf16[1,16,3,64,256]{4,3,2,1,0:T(8,128)(2,1)}) %reduce-scatter.6.cloned.1.call-update) | async-done | bytes 1572880 | tf_op jit(solution)/shard_map/reduce_scatter | solution.py:219
  371.8 3.8 convolution_bitcast_fusion.2
  381.4 3.5 copy.209
  385.3 3.5 copy.208
  391.9 18.0 %reduce-scatter.8.cloned.1.call-done = bf16[1,32,6144]{2,1,0:T(8,128)(2,1)} async-done(((bf16[4,32,6144]{2,1,0:T(8,128)(2,1)}), bf16[1,32,6144]{2,1,0:T(8,128)(2,1)}) %reduce-scatter.8.cloned.1.call-update) | async-done | bytes 393232 | tf_op jit(solution)/shard_map/reduce_scatter | solution.py:240
  (248 shorter events, 143.4 us)
Async XLA Ops:
  7.2 7.6 %copy-start = (bf16[128,2048]{1,0:T(8,128)(2,1)S(1)}, bf16[128,2048]{1,0:T(8,128)(2,1)}, u32[]{:S(2)}) copy-start(bf16[128,2048]{1,0:T(8,128)(2,1)} %param.14) | copy-start | bytes 1572868
  7.2 7.6 %copy-start.6 = (bf16[256,2048]{1,0:T(8,128)(2,1)S(1)}, bf16[256,2048]{1,0:T(8,128)(2,1)}, u32[]{:S(2)}) copy-start(bf16[256,2048]{1,0:T(8,128)(2,1)} %param.10) | copy-start | bytes 3145732
  7.2 8.6 %copy-start.31 = (bf16[64,16,3,256]{3,1,2,0:T(8,128)(2,1)S(1)}, bf16[64,16,3,256]{3,1,2,0:T(8,128)(2,1)}, u32[]{:S(2)}) copy-start(bf16[64,16,3,256]{3,1,2,0:T(8,128)(2,1)} %param.13) | copy-start | bytes 4718596
  7.2 71.7 %all-gather.5.cloned.1.call-start = ((), (), s32[]{:S(2)}) async-start(), calls=%async_computation.6 | async-start | bytes 3932160 | tf_op jit(solution)/shard_map/all_gather | solution.py:29
  9.5 137.5 %all-gather.7.cloned.1.call-start = ((), (), s32[]{:S(2)}) async-start(), calls=%async_computation.7 | async-start | bytes 3932160 | tf_op jit(solution)/shard_map/all_gather | solution.py:29
  11.8 6.5 %copy-start.39 = (s32[16,3]{0,1:T(4,128)S(1)}, s32[16,3]{0,1:T(4,128)}, u32[]{:S(2)}) copy-start(s32[16,3]{0,1:T(4,128)} %param.16) | copy-start | bytes 580
  11.8 6.5 %copy-start.40 = (s32[16,3]{0,1:T(4,128)S(1)}, s32[16,3]{0,1:T(4,128)}, u32[]{:S(2)}) copy-start(s32[16,3]{0,1:T(4,128)} %param.17) | copy-start | bytes 580
  11.8 41.0 %collective-permute-start.5 = (bf16[256,2048]{0,1:T(8,128)(2,1)}, bf16[256,2048]{0,1:T(8,128)(2,1)}, u32[]{:S(2)}, u32[]{:S(2)}) collective-permute-start(bf16[256,2048]{0,1:T(8,128)(2,1)} %copy.161), channel_id=1, source_target_pairs={{0,2},{2,0},{1,3},{3,1},{4,6},{6,4},{5,7},{7,5},{8,10},{10,8},{9,1... | collective-permute-start | bytes 3145736 | tf_op jit(solution)/shard_map/ppermute | solution.py:19
  14.8 47.4 %collective-permute-start.4 = (bf16[256,2048]{0,1:T(8,128)(2,1)}, bf16[256,2048]{0,1:T(8,128)(2,1)}, u32[]{:S(2)}, u32[]{:S(2)}) collective-permute-start(bf16[256,2048]{0,1:T(8,128)(2,1)} %copy.161), channel_id=1, source_target_pairs={{0,1},{1,0},{2,3},{3,2},{4,5},{5,4},{6,7},{7,6},{8,9},{9,8},{10,11... | collective-permute-start | bytes 3145736 | tf_op jit(solution)/shard_map/ppermute | solution.py:19
  15.2 28.1 %collective-permute-start.6 = (f32[256,128]{1,0:T(8,128)S(1)}, f32[256,128]{1,0:T(8,128)S(1)}, u32[]{:S(2)}, u32[]{:S(2)}) collective-permute-start(f32[256,128]{1,0:T(8,128)S(1)} %fusion.136), channel_id=1, source_target_pairs={{0,1},{1,0},{2,3},{3,2},{4,5},{5,4},{6,7},{7,6},{8,9},{9,8},{10,11... | collective-permute-start | bytes 393224 | tf_op jit(solution)/shard_map/ppermute | solution.py:19
  16.8 241.5 %reduce-scatter.4.cloned.1.call-start = ((), (), s32[]{:S(2)}) async-start(), calls=%async_computation.3 | async-start | bytes 7864320 | tf_op jit(solution)/shard_map/reduce_scatter | solution.py:184
  43.3 5.5 %collective-permute-start.7 = (f32[256,128]{1,0:T(8,128)S(1)}, f32[256,128]{1,0:T(8,128)S(1)}, u32[]{:S(2)}, u32[]{:S(2)}) collective-permute-start(f32[256,128]{1,0:T(8,128)S(1)} %add.171), channel_id=1, source_target_pairs={{0,2},{2,0},{1,3},{3,1},{4,6},{6,4},{5,7},{7,5},{8,10},{10,8},{9,1... | collective-permute-start | bytes 393224 | tf_op jit(solution)/shard_map/ppermute | solution.py:19
  78.9 6.3 %slice-start.2 = ((s8[6291456]{0:T(1024)(128)(4,1)}), s8[4194304]{0:T(1024)(128)(4,1)S(1)}, s32[]{:S(2)}) async-start(s8[6291456]{0:T(1024)(128)(4,1)} %bitcast.396), calls=%async_computation.10 | async-start | bytes 8388608
  83.5 16.3 %collective-permute-start.3 = (bf16[3,32,4,3,256]{4,1,3,2,0:T(8,128)(2,1)S(1)}, bf16[3,32,4,3,256]{4,1,3,2,0:T(8,128)(2,1)S(1)}, u32[]{:S(2)}, u32[]{:S(2)}) collective-permute-start(bf16[3,32,4,3,256]{4,1,3,2,0:T(8,128)(2,1)S(1)} %get-tuple-element.68), channel_id=1, source_target_pairs={{0,16},{16,0},{1,17},{17,1},{2,18},{18,2},{3,19},{19,3},{4,20},{20... | collective-permute-start | bytes 1769480 | tf_op jit(solution)/shard_map/ppermute | solution.py:54
  86.2 26.2 %collective-permute-start.2 = (bf16[3,32,4,3,256]{4,1,3,2,0:T(8,128)(2,1)S(1)}, bf16[3,32,4,3,256]{4,1,3,2,0:T(8,128)(2,1)S(1)}, u32[]{:S(2)}, u32[]{:S(2)}) collective-permute-start(bf16[3,32,4,3,256]{4,1,3,2,0:T(8,128)(2,1)S(1)} %get-tuple-element.66), channel_id=1, source_target_pairs={{0,16},{16,0},{1,17},{17,1},{2,18},{18,2},{3,19},{19,3},{4,20},{20... | collective-permute-start | bytes 1769480 | tf_op jit(solution)/shard_map/ppermute | solution.py:54
  86.8 38.3 %collective-permute-start.1 = (bf16[3,32,4,3,256]{4,1,3,2,0:T(8,128)(2,1)S(1)}, bf16[3,32,4,3,256]{4,1,3,2,0:T(8,128)(2,1)S(1)}, u32[]{:S(2)}, u32[]{:S(2)}) collective-permute-start(bf16[3,32,4,3,256]{4,1,3,2,0:T(8,128)(2,1)S(1)} %get-tuple-element.67), channel_id=1, source_target_pairs={{0,16},{16,0},{1,17},{17,1},{2,18},{18,2},{3,19},{19,3},{4,20},{20... | collective-permute-start | bytes 1769480 | tf_op jit(solution)/shard_map/ppermute | solution.py:54
  88.3 47.8 %collective-permute-start = (bf16[3,32,4,3,256]{4,1,3,2,0:T(8,128)(2,1)S(1)}, bf16[3,32,4,3,256]{4,1,3,2,0:T(8,128)(2,1)S(1)}, u32[]{:S(2)}, u32[]{:S(2)}) collective-permute-start(bf16[3,32,4,3,256]{4,1,3,2,0:T(8,128)(2,1)S(1)} %get-tuple-element.65), channel_id=1, source_target_pairs={{0,16},{16,0},{1,17},{17,1},{2,18},{18,2},{3,19},{19,3},{4,20},{20... | collective-permute-start | bytes 1769480 | tf_op jit(solution)/shard_map/ppermute | solution.py:54
  88.8 11.0 %copy-start.38 = (bf16[1,32,4,3,256]{4,1,3,2,0:T(8,128)(2,1)S(1)}, bf16[1,32,4,3,256]{4,1,3,2,0:T(8,128)(2,1)}, u32[]{:S(2)}) copy-start(bf16[1,32,4,3,256]{4,1,3,2,0:T(8,128)(2,1)} %get-tuple-element.110) | copy-start | bytes 589828
  88.8 11.5 %copy-start.20 = (f32[16,256,256]{1,2,0:T(8,128)S(1)}, f32[16,256,256]{1,2,0:T(8,128)}, u32[]{:S(2)}) copy-start(f32[16,256,256]{1,2,0:T(8,128)} %convolution_bitcast_fusion.3) | copy-start | bytes 12582916
  104.2 8.3 %copy-start.36 = (bf16[1,32,4,3,256]{4,1,3,2,0:T(8,128)(2,1)S(1)}, bf16[1,32,4,3,256]{4,1,3,2,0:T(8,128)(2,1)}, u32[]{:S(2)}) copy-start(bf16[1,32,4,3,256]{4,1,3,2,0:T(8,128)(2,1)} %get-tuple-element.111) | copy-start | bytes 589828
  117.2 7.9 %copy-start.37 = (bf16[1,32,4,3,256]{4,1,3,2,0:T(8,128)(2,1)S(1)}, bf16[1,32,4,3,256]{4,1,3,2,0:T(8,128)(2,1)}, u32[]{:S(2)}) copy-start(bf16[1,32,4,3,256]{4,1,3,2,0:T(8,128)(2,1)} %get-tuple-element.112) | copy-start | bytes 589828
  125.6 10.5 %copy-start.35 = (bf16[1,32,4,3,256]{4,1,3,2,0:T(8,128)(2,1)S(1)}, bf16[1,32,4,3,256]{4,1,3,2,0:T(8,128)(2,1)}, u32[]{:S(2)}) copy-start(bf16[1,32,4,3,256]{4,1,3,2,0:T(8,128)(2,1)} %get-tuple-element.113) | copy-start | bytes 589828
  147.0 224.8 %reduce-scatter.6.cloned.1.call-start = ((), (), s32[]{:S(2)}) async-start(), calls=%async_computation.4 | async-start | bytes 7864320 | tf_op jit(solution)/shard_map/reduce_scatter | solution.py:219
  154.9 16.3 %collective-permute-start.11 = (bf16[3,32,4,3,256]{4,1,0,3,2:T(8,128)(2,1)S(1)}, bf16[3,32,4,3,256]{4,1,0,3,2:T(8,128)(2,1)S(1)}, u32[]{:S(2)}, u32[]{:S(2)}) collective-permute-start(bf16[3,32,4,3,256]{4,1,0,3,2:T(8,128)(2,1)S(1)} %get-tuple-element.64), channel_id=1, source_target_pairs={{0,16},{16,0},{1,17},{17,1},{2,18},{18,2},{3,19},{19,3},{4,20},{20... | collective-permute-start | bytes 1769480 | tf_op jit(solution)/shard_map/ppermute | solution.py:54
  156.6 27.2 %collective-permute-start.10 = (bf16[3,32,4,3,256]{4,1,0,3,2:T(8,128)(2,1)S(1)}, bf16[3,32,4,3,256]{4,1,0,3,2:T(8,128)(2,1)S(1)}, u32[]{:S(2)}, u32[]{:S(2)}) collective-permute-start(bf16[3,32,4,3,256]{4,1,0,3,2:T(8,128)(2,1)S(1)} %get-tuple-element.62), channel_id=1, source_target_pairs={{0,16},{16,0},{1,17},{17,1},{2,18},{18,2},{3,19},{19,3},{4,20},{20... | collective-permute-start | bytes 1769480 | tf_op jit(solution)/shard_map/ppermute | solution.py:54
  157.3 39.2 %collective-permute-start.9 = (bf16[3,32,4,3,256]{4,1,0,3,2:T(8,128)(2,1)S(1)}, bf16[3,32,4,3,256]{4,1,0,3,2:T(8,128)(2,1)S(1)}, u32[]{:S(2)}, u32[]{:S(2)}) collective-permute-start(bf16[3,32,4,3,256]{4,1,0,3,2:T(8,128)(2,1)S(1)} %get-tuple-element.63), channel_id=1, source_target_pairs={{0,16},{16,0},{1,17},{17,1},{2,18},{18,2},{3,19},{19,3},{4,20},{20... | collective-permute-start | bytes 1769480 | tf_op jit(solution)/shard_map/ppermute | solution.py:54
  159.0 47.7 %collective-permute-start.8 = (bf16[3,32,4,3,256]{4,1,0,3,2:T(8,128)(2,1)S(1)}, bf16[3,32,4,3,256]{4,1,0,3,2:T(8,128)(2,1)S(1)}, u32[]{:S(2)}, u32[]{:S(2)}) collective-permute-start(bf16[3,32,4,3,256]{4,1,0,3,2:T(8,128)(2,1)S(1)} %get-tuple-element.61), channel_id=1, source_target_pairs={{0,16},{16,0},{1,17},{17,1},{2,18},{18,2},{3,19},{19,3},{4,20},{20... | collective-permute-start | bytes 1769480 | tf_op jit(solution)/shard_map/ppermute | solution.py:54
  258.4 151.6 %reduce-scatter.8.cloned.1.call-start = ((), (), s32[]{:S(2)}) async-start(), calls=%async_computation.5 | async-start | bytes 1966080 | tf_op jit(solution)/shard_map/reduce_scatter | solution.py:240
  292.5 18.1 %collective-permute-start.12 = (f32[256,128]{1,0:T(8,128)S(1)}, f32[256,128]{1,0:T(8,128)S(1)}, u32[]{:S(2)}, u32[]{:S(2)}) collective-permute-start(f32[256,128]{1,0:T(8,128)S(1)} %convolution_bitcast_fusion.20), channel_id=1, source_target_pairs={{0,1},{1,0},{2,3},{3,2},{4,5},{5,4},{6,7},{7,6},{8,9},{9,8},{10,11... | collective-permute-start | bytes 393224 | tf_op jit(solution)/shard_map/ppermute | solution.py:19
  303.3 14.7 %collective-permute-start.14 = (bf16[256,2048]{1,0:T(8,128)(2,1)}, bf16[256,2048]{1,0:T(8,128)(2,1)}, u32[]{:S(2)}, u32[]{:S(2)}) collective-permute-start(bf16[256,2048]{1,0:T(8,128)(2,1)} %bitcast.173), channel_id=1, source_target_pairs={{0,1},{1,0},{2,3},{3,2},{4,5},{5,4},{6,7},{7,6},{8,9},{9,8},{10,11... | collective-permute-start | bytes 3145736 | tf_op jit(solution)/shard_map/ppermute | solution.py:19
  310.6 5.5 %collective-permute-start.13 = (f32[256,128]{1,0:T(8,128)S(1)}, f32[256,128]{1,0:T(8,128)S(1)}, u32[]{:S(2)}, u32[]{:S(2)}) collective-permute-start(f32[256,128]{1,0:T(8,128)S(1)} %add.196), channel_id=1, source_target_pairs={{0,2},{2,0},{1,3},{3,1},{4,6},{6,4},{5,7},{7,5},{8,10},{10,8},{9,1... | collective-permute-start | bytes 393224 | tf_op jit(solution)/shard_map/ppermute | solution.py:19
  315.5 25.1 %collective-permute-start.15 = (bf16[256,2048]{1,0:T(8,128)(2,1)}, bf16[256,2048]{1,0:T(8,128)(2,1)}, u32[]{:S(2)}, u32[]{:S(2)}) collective-permute-start(bf16[256,2048]{1,0:T(8,128)(2,1)} %bitcast.175), channel_id=1, source_target_pairs={{0,2},{2,0},{1,3},{3,1},{4,6},{6,4},{5,7},{7,5},{8,10},{10,8},{9,1... | collective-permute-start | bytes 3145736 | tf_op jit(solution)/shard_map/ppermute | solution.py:19
  (37 other events, 126.2 us)
Sparse Core Ops, SparseCore 0:
  9.6 66.1 all-gather.4
  77.4 62.0 all-gather.6
  147.2 111.1 reduce-scatter.3
  260.5 111.2 reduce-scatter.5
  374.0 35.9 reduce-scatter.7

commit v2 on v0

--- a/solution.py
+++ b/solution.py
@@ -216,7 +216,6 @@
         "htj,rhj->tr", grad_blocks, right_blocks, preferred_element_type=jnp.float32
     )
     back_low = butterfly_sum(back_part, "tensor").astype(jnp.bfloat16)
-    up_summed = lax.psum_scatter(up_parts, "dp", scatter_dimension=0, tiled=False)
     left_parts = jnp.stack(
         split_rows(
             lax.dot_general(
@@ -236,8 +235,14 @@
         )
     )
     joined = (jnp.concatenate([left_parts, right_parts], axis=2) * inv_root).astype(jnp.bfloat16)
-    joined, up_summed, incoming = lax.optimization_barrier((joined, up_summed, incoming))
-    joined = lax.psum_scatter(joined, "dp", scatter_dimension=0, tiled=False).astype(jnp.float32)
+    lane = up_parts.shape[-1]
+    both = jnp.concatenate(
+        [up_parts.reshape(dp_size, -1, lane), joined.reshape(dp_size, -1, lane)], axis=1
+    )
+    both = lax.psum_scatter(both, "dp", scatter_dimension=0, tiled=False)
+    up_size = math.prod(up_parts.shape[1:]) // lane
+    up_summed = both[:up_size].reshape(up_parts.shape[1:])
+    joined = both[up_size:].reshape(joined.shape[1:]).astype(jnp.float32)
     grad_up = jnp.transpose(up_summed.astype(jnp.float32), (2, 0, 1, 3))
     own_term = section_term(0)
     for level_bit in range(section_count - 1):

time: 427 us -> 423 us (level)
  waiting for transfers between devices: 196 us -> 187 us
  other arithmetic: 41.3 us -> 47.2 us
    reduce_scatter x2 -> x1, waiting for transfers between devices: 49.8 us -> 79.6 us  [shards(): both = lax.psum_scatter(both, 'dp', scatter_dimension=0, tiled=False)]
    reduce_scatter x1, waiting for transfers between devices: 34.6 us -> 7.82 us  [shards(): lax.psum_scatter(down_parts, 'dp', scatter_dimension=0, tiled=False)]
    ppermute x8, waiting for transfers between devices: 26.6 us -> 11.7 us  [swapped(): return lax.ppermute(block, axis, route)]
    concatenate x0 -> x1, other arithmetic: none -> 6.91 us  [shards(): jnp.concatenate([up_parts.reshape(dp_size, -1, lane), joined.reshape(dp_s...]
  transfers between devices with their start and end apart: 17 -> 16, of which waited for: 10 -> 9; matrix products, arithmetic and copies ran while one was open for 43% -> 42% of each run, Pallas kernels for 0% -> 0%
where the time goes in v2:
time: 423 us; the launch traced here: 417 us
  waiting for transfers between devices  187 us (44%)
  local copies, waits for them, and re-layouts  105 us (25%)
  matrix products  50 us (12%)
  other arithmetic  47.2 us (11%)
  between operations  15.2 us (4%)
  starting transfers between devices  12.9 us (3%)
    ppermute x4, waiting for transfers between devices, swap_shares(): lax.ppermute(send[:, :, half * width:(half + 1) * width], 'groups', [(0,...  83.8 us
    reduce_scatter x1, waiting for transfers between devices, shards(): both = lax.psum_scatter(both, 'dp', scatter_dimension=0, tiled=False)  79.6 us
    gather x9, local copies, waits for them, and re-layouts, pick_blocks(): picked.append(jnp.take(shaped, pattern[:, which_section], axis=1))  24.3 us
    unnamed x93, local copies, waits for them, and re-layouts  20.9 us
    transpose x3, local copies, waits for them, and re-layouts, section_term(): jnp.einsum('htj,ihj->thi', grad_blocks, up_full[:, :, which_section, :],...  12.7 us
    dot_general x2, matrix products, shards(): jnp.einsum('thskr,krhsj->htj', other_rows[:, lo:hi], piece, preferred_ele...  12.6 us
    ppermute x8, waiting for transfers between devices, swapped(): return lax.ppermute(block, axis, route)  11.7 us
    slice x5, local copies, waits for them, and re-layouts, split_rows(): lax.slice_in_dim(values, d * rows, (d + 1) * rows, axis=axis)  8.7 us
  transfers between devices with their start and end apart: 16, of which 9 were waited for; matrix products, arithmetic and copies ran while one was open for 42% of the time, Pallas kernels for 0%

profile of v2, /device:TPU:0, one launch (start us, length us, event | category | flops | bytes accessed | tf_op | source)
XLA Modules:
  0.0 417.0 jit_solution(6018891468729681806)
XLA Ops:
  19.9 4.1 copy.142
  31.2 3.4 broadcast_select_fusion.2
  39.6 3.6 pad_maximum_fusion.1
  44.6 5.4 %collective-permute-done.5 = f32[256,128]{1,0:T(8,128)S(1)} collective-permute-done((f32[256,128]{1,0:T(8,128)S(1)}, f32[256,128]{1,0:T(8,128)S(1)}, u32[]{:S(2)}, u32[]{:S(2)}) %collective-permute-start.5) | collective-permute-done | bytes 131104 | tf_op jit(solution)/shard_map/ppermute | solution.py:19
  62.2 3.2 gather_fusion.4
  65.4 4.1 copy.145
  72.1 3.7 all-gather.5.cloned.1.call-done
  75.8 3.1 copy.130
  87.6 21.6 %collective-permute-done.1 = bf16[3,32,8,3,256]{4,1,3,2,0:T(8,128)(2,1)S(1)} collective-permute-done((bf16[3,32,8,3,256]{4,1,3,2,0:T(8,128)(2,1)S(1)}, bf16[3,32,8,3,256]{4,1,3,2,0:T(8,128)(2,1)S(1)}, u32[]{:S(2)}, u32[]{:S(2)}) %collective-permute-start.1) | collective-permute-done | bytes 1179680 | tf_op jit(solution)/shard_map/ppermute | solution.py:54
  110.2 6.5 %multiply_convert_fusion = (bf16[8,256,256]{1,2,0:T(8,128)(2,1)S(1)}, f32[8,256,256]{1,2,0:T(8,128)}) fusion(f32[16,256,256]{1,2,0:T(8,128)S(1)} %copy-done.25, bf16[4,32,8,3,256]{4,1,3,2,0:T(8,128)(2,1)S(1)} %fusion.73, bf16[256,16,3,4,1,32]{0,5,4,3,1,2:T(8,128)(2,1)S(1)} %get-tuple-element.49, f32[16,256,256]{1,2,0:T(8,128)S(1)} %fusion.15), kind=kOutput, calls=%fused_computation.104 | convolution fusion | flops 413663232 | bytes 12058624 | tf_op jit(solution)/shard_map/thskr,krhsj->htj/dot_general | solution.py:154
  117.3 15.8 %collective-permute-done = bf16[3,32,8,3,256]{4,1,3,2,0:T(8,128)(2,1)S(1)} collective-permute-done((bf16[3,32,8,3,256]{4,1,3,2,0:T(8,128)(2,1)S(1)}, bf16[3,32,8,3,256]{4,1,3,2,0:T(8,128)(2,1)S(1)}, u32[]{:S(2)}, u32[]{:S(2)}) %collective-permute-start) | collective-permute-done | bytes 1179680 | tf_op jit(solution)/shard_map/ppermute | solution.py:54
  136.2 6.1 %multiply_convert_fusion.1 = (bf16[8,256,256]{1,2,0:T(8,128)(2,1)S(1)}, f32[8,256,256]{1,2,0:T(8,128)}) fusion(f32[16,256,256]{1,2,0:T(8,128)S(1)} %copy-done.25, bf16[4,32,8,3,256]{4,1,3,2,0:T(8,128)(2,1)S(1)} %fusion.76, bf16[256,16,3,4,1,32]{0,5,4,3,1,2:T(8,128)(2,1)S(1)} %get-tuple-element.49, f32[16,256,256]{1,2,0:T(8,128)S(1)} %fusion.15), kind=kOutput, calls=%fused_computation.105 | convolution fusion | flops 413663232 | bytes 12058624 | tf_op jit(solution)/shard_map/thskr,krhsj->htj/dot_general | solution.py:154
  145.0 4.0 fusion
  159.7 24.2 %collective-permute-done.7 = bf16[3,32,8,3,256]{4,1,0,3,2:T(8,128)(2,1)S(1)} collective-permute-done((bf16[3,32,8,3,256]{4,1,0,3,2:T(8,128)(2,1)S(1)}, bf16[3,32,8,3,256]{4,1,0,3,2:T(8,128)(2,1)S(1)}, u32[]{:S(2)}, u32[]{:S(2)}) %collective-permute-start.7) | collective-permute-done | bytes 1179680 | tf_op jit(solution)/shard_map/ppermute | solution.py:54
  184.8 22.3 %collective-permute-done.6 = bf16[3,32,8,3,256]{4,1,0,3,2:T(8,128)(2,1)S(1)} collective-permute-done((bf16[3,32,8,3,256]{4,1,0,3,2:T(8,128)(2,1)S(1)}, bf16[3,32,8,3,256]{4,1,0,3,2:T(8,128)(2,1)S(1)}, u32[]{:S(2)}, u32[]{:S(2)}) %collective-permute-start.6) | collective-permute-done | bytes 1179680 | tf_op jit(solution)/shard_map/ppermute | solution.py:54
  208.4 3.7 fusion.4
  212.2 5.3 %fusion.8 = bf16[16,256,256]{1,2,0:T(8,128)(2,1)S(1)} fusion(f32[8,256,256]{1,2,0:T(8,128)} %get-tuple-element.64, f32[8,256,256]{1,2,0:T(8,128)} %get-tuple-element.62, bf16[256,16,3,256]{3,0,2,1:T(8,128)(2,1)S(1)} %bitcast.286, bf16[256,16,1,256]{3,0,2,1:T(8,128)(2,1)S(1)} %copy-done.14, bf16[256,16,1,256]{3,0,2,1:T(8,128)(2,1)S(1)} %copy-done.16, ...), kind=kOutput, calls=%fused_computation.33 | convolution fusion | flops 1620049920 | bytes 18874368 | tf_op jit(solution)/shard_map/thso,jhso->htj/dot_general | solution.py:185
  221.8 4.2 %fusion.1 = bf16[4,16,3,64,256]{4,3,2,1,0:T(8,128)(2,1)} fusion(f32[1,16,3,64,256]{4,3,2,1,0:T(8,128)S(1)} %fusion.62, f32[1,16,3,64,256]{4,3,2,1,0:T(8,128)S(1)} %fusion.59, f32[1,16,3,64,256]{4,3,2,1,0:T(8,128)S(1)} %fusion.56, f32[1,16,3,64,256]{4,3,2,1,0:T(8,128)S(1)} %fusion.53), kind=kLoop, calls=%fused_computation.17 | loop fusion | flops 15728640 | bytes 18874368 | tf_op jit(solution)/shard_map/convert_element_type | solution.py:212
  247.3 3.6 convert_element_type.86
  250.9 7.8 %reduce-scatter.3.cloned.1.call-done = bf16[1,16,64,3,256]{4,2,3,1,0:T(8,128)(2,1)} async-done(((bf16[4,16,64,3,256]{4,2,3,1,0:T(8,128)(2,1)}), bf16[1,16,64,3,256]{4,2,3,1,0:T(8,128)(2,1)}) %reduce-scatter.3.cloned.1.call-update) | async-done | bytes 1572880 | tf_op jit(solution)/shard_map/reduce_scatter | solution.py:184
  258.7 6.9 %pad_maximum_fusion = bf16[4,3840,256]{2,1,0:T(8,128)(2,1)} fusion(bf16[4,768,256]{2,1,0:T(8,128)(2,1)} %convert_element_type.86, bf16[4,3072,256]{2,1,0:T(8,128)(2,1)} %bitcast.280), kind=kLoop, calls=%fused_computation.18 | loop fusion | flops 15728640 | bytes 15728640 | tf_op jit(solution)/shard_map/concatenate | solution.py:239
  265.7 3.2 copy.133
  269.2 4.6 %fusion.7 = bf16[4,2,32,16,3,256]{5,2,4,3,0,1:T(8,128)(2,1)S(1)} fusion(s32[]{:T(128)S(6)} %select_n.61, bf16[4,1,32,16,3,256]{5,2,4,3,0,1:T(8,128)(2,1)S(1)} %maximum_bitcast_fusion, bf16[4,1,32,16,3,256]{5,2,4,3,0,1:T(8,128)(2,1)S(1)} %copy.133), kind=kLoop, calls=%fused_computation.24 | loop fusion | flops 9437184 | bytes 12582916 | tf_op jit(solution)/shard_map/concatenate | solution.py:68
  273.9 3.9 copy.135
  282.7 4.6 %copy.170 = bf16[256,16,256]{2,1,0:T(8,128)(2,1)} copy(bf16[256,16,256]{0,2,1:T(8,128)(2,1)} %convolution_bitcast_fusion) | data formatting | bytes 4194304 | tf_op jit(solution)/shard_map/htj,ihj->thi/transpose | solution.py:198
  294.4 4.8 %copy.167 = bf16[256,16,256]{2,1,0:T(8,128)(2,1)} copy(bf16[256,16,256]{0,2,1:T(8,128)(2,1)} %convolution_bitcast_fusion.1) | data formatting | bytes 4194304 | tf_op jit(solution)/shard_map/htj,ihj->thi/transpose | solution.py:198
  304.9 3.3 copy.164
  309.6 6.3 %collective-permute-done.9 = bf16[256,2048]{1,0:T(8,128)(2,1)} collective-permute-done((bf16[256,2048]{1,0:T(8,128)(2,1)}, bf16[256,2048]{1,0:T(8,128)(2,1)}, u32[]{:S(2)}, u32[]{:S(2)}) %collective-permute-start.9) | collective-permute-done | bytes 1048608 | tf_op jit(solution)/shard_map/ppermute | solution.py:19
  315.9 3.2 add_convert_fusion
  319.5 3.5 copy.184
  323.0 79.6 %reduce-scatter.5.cloned.1.call-done = bf16[1,3840,256]{2,1,0:T(8,128)(2,1)} async-done(((bf16[4,3840,256]{2,1,0:T(8,128)(2,1)}), bf16[1,3840,256]{2,1,0:T(8,128)(2,1)}) %reduce-scatter.5.cloned.1.call-update) | async-done | bytes 1966096 | tf_op jit(solution)/shard_map/reduce_scatter | solution.py:242
  406.5 3.5 copy.183
  (214 shorter events, 118.8 us)
Async XLA Ops:
  7.2 6.7 %copy-start = (bf16[128,2048]{1,0:T(8,128)(2,1)S(1)}, bf16[128,2048]{1,0:T(8,128)(2,1)}, u32[]{:S(2)}) copy-start(bf16[128,2048]{1,0:T(8,128)(2,1)} %param.14) | copy-start | bytes 1572868
  7.2 68.6 %all-gather.5.cloned.1.call-start = ((), (), s32[]{:S(2)}) async-start(), calls=%async_computation.4 | async-start | bytes 3932160 | tf_op jit(solution)/shard_map/all_gather | solution.py:29
  9.5 5.4 %copy-start.31 = (bf16[64,16,3,256]{3,1,2,0:T(8,128)(2,1)S(1)}, bf16[64,16,3,256]{3,1,2,0:T(8,128)(2,1)}, u32[]{:S(2)}) copy-start(bf16[64,16,3,256]{3,1,2,0:T(8,128)(2,1)} %param.13) | copy-start | bytes 4718596
  9.5 139.4 %all-gather.7.cloned.1.call-start = ((), (), s32[]{:S(2)}) async-start(), calls=%async_computation.5 | async-start | bytes 3932160 | tf_op jit(solution)/shard_map/all_gather | solution.py:29
  10.8 42.0 %collective-permute-start.3 = (bf16[256,2048]{0,1:T(8,128)(2,1)}, bf16[256,2048]{0,1:T(8,128)(2,1)}, u32[]{:S(2)}, u32[]{:S(2)}) collective-permute-start(bf16[256,2048]{0,1:T(8,128)(2,1)} %copy.140), channel_id=1, source_target_pairs={{0,2},{2,0},{1,3},{3,1},{4,6},{6,4},{5,7},{7,5},{8,10},{10,8},{9,1... | collective-permute-start | bytes 3145736 | tf_op jit(solution)/shard_map/ppermute | solution.py:19
  13.8 45.4 %collective-permute-start.2 = (bf16[256,2048]{0,1:T(8,128)(2,1)}, bf16[256,2048]{0,1:T(8,128)(2,1)}, u32[]{:S(2)}, u32[]{:S(2)}) collective-permute-start(bf16[256,2048]{0,1:T(8,128)(2,1)} %copy.140), channel_id=1, source_target_pairs={{0,1},{1,0},{2,3},{3,2},{4,5},{5,4},{6,7},{7,6},{8,9},{9,8},{10,11... | collective-permute-start | bytes 3145736 | tf_op jit(solution)/shard_map/ppermute | solution.py:19
  14.3 29.1 %collective-permute-start.4 = (f32[256,128]{1,0:T(8,128)S(1)}, f32[256,128]{1,0:T(8,128)}, u32[]{:S(2)}, u32[]{:S(2)}) collective-permute-start(f32[256,128]{1,0:T(8,128)S(1)} %fusion.124), channel_id=1, source_target_pairs={{0,1},{1,0},{2,3},{3,2},{4,5},{5,4},{6,7},{7,6},{8,9},{9,8},{10,11... | collective-permute-start | bytes 393224 | tf_op jit(solution)/shard_map/ppermute | solution.py:19
  15.8 242.9 %reduce-scatter.3.cloned.1.call-start = ((), (), s32[]{:S(2)}) async-start(), calls=%async_computation.2 | async-start | bytes 7864320 | tf_op jit(solution)/shard_map/reduce_scatter | solution.py:184
  19.9 4.1 copy-start.34
  34.9 4.7 %copy-start.13 = (bf16[256,16,1,256]{3,0,2,1:T(8,128)(2,1)}, bf16[256,16,1,256]{3,0,2,1:T(8,128)(2,1)S(1)}, u32[]{:S(2)}) copy-start(bf16[256,16,1,256]{3,0,2,1:T(8,128)(2,1)S(1)} %select_bitcast_fusion) | copy-start | bytes 6291460
  39.6 4.9 %copy-start.39 = (s32[16]{0:T(128)S(1)}, s32[16]{0:T(128)}, u32[]{:S(2)}) copy-start(s32[16]{0:T(128)} %get-tuple-element.81) | copy-start | bytes 196
  39.6 5.0 %copy-start.38 = (s32[16]{0:T(128)S(1)}, s32[16]{0:T(128)}, u32[]{:S(2)}) copy-start(s32[16]{0:T(128)} %get-tuple-element.83) | copy-start | bytes 196
  43.2 6.8 %copy-start.35 = (bf16[128,4096]{1,0:T(8,128)(2,1)S(1)}, bf16[128,4096]{1,0:T(8,128)(2,1)}, u32[]{:S(2)}) copy-start(bf16[128,4096]{1,0:T(8,128)(2,1)} %param.15) | copy-start | bytes 3145732
  44.4 5.5 %collective-permute-start.5 = (f32[256,128]{1,0:T(8,128)S(1)}, f32[256,128]{1,0:T(8,128)S(1)}, u32[]{:S(2)}, u32[]{:S(2)}) collective-permute-start(f32[256,128]{1,0:T(8,128)S(1)} %add.123), channel_id=1, source_target_pairs={{0,2},{2,0},{1,3},{3,1},{4,6},{6,4},{5,7},{7,5},{8,10},{10,8},{9,1... | collective-permute-start | bytes 393224 | tf_op jit(solution)/shard_map/ppermute | solution.py:19
  59.2 10.3 %copy-start.3 = (bf16[16,256,256]{1,2,0:T(8,128)(2,1)}, bf16[16,256,256]{1,2,0:T(8,128)(2,1)S(1)}, u32[]{:S(2)}) copy-start(bf16[16,256,256]{1,2,0:T(8,128)(2,1)S(1)} %copy.148) | copy-start | bytes 6291460
  80.3 28.9 %collective-permute-start.1 = (bf16[3,32,8,3,256]{4,1,3,2,0:T(8,128)(2,1)S(1)}, bf16[3,32,8,3,256]{4,1,3,2,0:T(8,128)(2,1)S(1)}, u32[]{:S(2)}, u32[]{:S(2)}) collective-permute-start(bf16[3,32,8,3,256]{4,1,3,2,0:T(8,128)(2,1)S(1)} %get-tuple-element.56), channel_id=1, source_target_pairs={{0,16},{16,0},{1,17},{17,1},{2,18},{18,2},{3,19},{19,3},{4,20},{20... | collective-permute-start | bytes 3538952 | tf_op jit(solution)/shard_map/ppermute | solution.py:54
  83.7 49.5 %collective-permute-start = (bf16[3,32,8,3,256]{4,1,3,2,0:T(8,128)(2,1)S(1)}, bf16[3,32,8,3,256]{4,1,3,2,0:T(8,128)(2,1)S(1)}, u32[]{:S(2)}, u32[]{:S(2)}) collective-permute-start(bf16[3,32,8,3,256]{4,1,3,2,0:T(8,128)(2,1)S(1)} %get-tuple-element.55), channel_id=1, source_target_pairs={{0,16},{16,0},{1,17},{17,1},{2,18},{18,2},{3,19},{19,3},{4,20},{20... | collective-permute-start | bytes 3538952 | tf_op jit(solution)/shard_map/ppermute | solution.py:54
  85.2 25.0 %copy-start.25 = (f32[16,256,256]{1,2,0:T(8,128)S(1)}, f32[16,256,256]{1,2,0:T(8,128)}, u32[]{:S(2)}) copy-start(f32[16,256,256]{1,2,0:T(8,128)} %convolution_bitcast_fusion.3) | copy-start | bytes 12582916
  109.2 7.5 %slice-start = ((s8[6291456]{0:T(1024)(128)(4,1)}), s8[4194304]{0:T(1024)(128)(4,1)S(1)}, s32[]{:S(2)}) async-start(s8[6291456]{0:T(1024)(128)(4,1)} %bitcast.273), calls=%async_computation.6 | async-start | bytes 8388608
  110.2 6.5 %copy-start.21 = (bf16[4,32,8,3,256]{4,1,3,2,0:T(8,128)(2,1)}, bf16[4,32,8,3,256]{4,1,3,2,0:T(8,128)(2,1)S(1)}, u32[]{:S(2)}) copy-start(bf16[4,32,8,3,256]{4,1,3,2,0:T(8,128)(2,1)S(1)} %fusion.73) | copy-start | bytes 4718596
  110.2 6.5 %slice-start.1 = ((s8[6291456]{0:T(1024)(128)(4,1)}), s8[2097152]{0:T(1024)(128)(4,1)S(1)}, s32[]{:S(2)}) async-start(s8[6291456]{0:T(1024)(128)(4,1)} %bitcast.273), calls=%async_computation.7 | async-start | bytes 4194304
  149.0 253.6 %reduce-scatter.5.cloned.1.call-start = ((), (), s32[]{:S(2)}) async-start(), calls=%async_computation.3 | async-start | bytes 9830400 | tf_op jit(solution)/shard_map/reduce_scatter | solution.py:242
  155.0 28.9 %collective-permute-start.7 = (bf16[3,32,8,3,256]{4,1,0,3,2:T(8,128)(2,1)S(1)}, bf16[3,32,8,3,256]{4,1,0,3,2:T(8,128)(2,1)S(1)}, u32[]{:S(2)}, u32[]{:S(2)}) collective-permute-start(bf16[3,32,8,3,256]{4,1,0,3,2:T(8,128)(2,1)S(1)} %get-tuple-element.54), channel_id=1, source_target_pairs={{0,16},{16,0},{1,17},{17,1},{2,18},{18,2},{3,19},{19,3},{4,20},{20... | collective-permute-start | bytes 3538952 | tf_op jit(solution)/shard_map/ppermute | solution.py:54
  156.7 50.4 %collective-permute-start.6 = (bf16[3,32,8,3,256]{4,1,0,3,2:T(8,128)(2,1)S(1)}, bf16[3,32,8,3,256]{4,1,0,3,2:T(8,128)(2,1)S(1)}, u32[]{:S(2)}, u32[]{:S(2)}) collective-permute-start(bf16[3,32,8,3,256]{4,1,0,3,2:T(8,128)(2,1)S(1)} %get-tuple-element.53), channel_id=1, source_target_pairs={{0,16},{16,0},{1,17},{17,1},{2,18},{18,2},{3,19},{19,3},{4,20},{20... | collective-permute-start | bytes 3538952 | tf_op jit(solution)/shard_map/ppermute | solution.py:54
  208.4 3.8 copy-start.14
  208.4 3.8 copy-start.16
  212.2 5.4 %copy-start.36 = (bf16[128,4096]{1,0:T(8,128)(2,1)S(1)}, bf16[128,4096]{1,0:T(8,128)(2,1)}, u32[]{:S(2)}) copy-start(bf16[128,4096]{1,0:T(8,128)(2,1)} %param.15) | copy-start | bytes 3145732
  218.3 8.5 %collective-permute-start.10 = (f32[256,128]{1,0:T(8,128)S(1)}, f32[256,128]{1,0:T(8,128)S(1)}, u32[]{:S(2)}, u32[]{:S(2)}) collective-permute-start(f32[256,128]{1,0:T(8,128)S(1)} %convolution_bitcast_fusion.4), channel_id=1, source_target_pairs={{0,1},{1,0},{2,3},{3,2},{4,5},{5,4},{6,7},{7,6},{8,9},{9,8},{10,11... | collective-permute-start | bytes 393224 | tf_op jit(solution)/shard_map/ppermute | solution.py:19
  226.8 17.2 %collective-permute-start.11 = (f32[256,128]{1,0:T(8,128)S(1)}, f32[256,128]{1,0:T(8,128)S(1)}, u32[]{:S(2)}, u32[]{:S(2)}) collective-permute-start(f32[256,128]{1,0:T(8,128)S(1)} %add.138), channel_id=1, source_target_pairs={{0,2},{2,0},{1,3},{3,1},{4,6},{6,4},{5,7},{7,5},{8,10},{10,8},{9,1... | collective-permute-start | bytes 393224 | tf_op jit(solution)/shard_map/ppermute | solution.py:19
  287.3 4.9 %copy-start.12 = (bf16[256,16,256]{2,1,0:T(8,128)(2,1)S(1)}, bf16[256,16,256]{2,1,0:T(8,128)(2,1)}, u32[]{:S(2)}) copy-start(bf16[256,16,256]{2,1,0:T(8,128)(2,1)} %get-tuple-element.46) | copy-start | bytes 6291460
  290.8 25.1 %collective-permute-start.9 = (bf16[256,2048]{1,0:T(8,128)(2,1)}, bf16[256,2048]{1,0:T(8,128)(2,1)}, u32[]{:S(2)}, u32[]{:S(2)}) collective-permute-start(bf16[256,2048]{1,0:T(8,128)(2,1)} %bitcast.133), channel_id=1, source_target_pairs={{0,2},{2,0},{1,3},{3,1},{4,6},{6,4},{5,7},{7,5},{8,10},{10,8},{9,1... | collective-permute-start | bytes 3145736 | tf_op jit(solution)/shard_map/ppermute | solution.py:19
  302.7 13.2 %collective-permute-start.8 = (bf16[256,2048]{1,0:T(8,128)(2,1)}, bf16[256,2048]{1,0:T(8,128)(2,1)}, u32[]{:S(2)}, u32[]{:S(2)}) collective-permute-start(bf16[256,2048]{1,0:T(8,128)(2,1)} %bitcast.131), channel_id=1, source_target_pairs={{0,1},{1,0},{2,3},{3,2},{4,5},{5,4},{6,7},{7,6},{8,9},{9,8},{10,11... | collective-permute-start | bytes 3145736 | tf_op jit(solution)/shard_map/ppermute | solution.py:19
  (28 other events, 69.6 us)
Sparse Core Ops, SparseCore 0:
  9.6 66.1 all-gather.4
  77.4 62.0 all-gather.6
  149.1 109.6 reduce-scatter.2
  265.8 136.7 reduce-scatter.4
